TPU v7x, 32 devices: a whole 2x2x4 slice. The times are simulated.
32 devices in a mesh: dp: 4 (over x, core), tensor: 8 (over z, y).
Axes of the slice: x: 2, y: 2, z: 4, core: 2. Of those that a mesh axis runs over, the one named last changes fastest.
Arguments:
- grad: bfloat16 [4, 576, 6144], P('dp', 'tensor'), as said below
- momentum: float32 [4, 576, 6144], P('dp', 'tensor'), may hold values from -6 to 6
- owner: int32 [4], replicated, may hold values from 0 to 3, each once
Outputs:
- update: bfloat16 [4, 576, 6144], P(None, 'tensor')
- new_momentum: float32 [4, 576, 6144], P('dp', 'tensor')
Inputs may be any that keep to these rules, and one draw needn't show every extreme that they name: owner names each matrix 0 to 3 exactly once. `grad`: gradient entries are finite; every matrix has full rank.
All inputs are finite; a program needn't handle non-finite values.
Results may differ from a plain program's by a relative error of at most 0.0013.
The roundings to bfloat16 on the way count: a program that leaves them out, or rounds other values in their place, can miss the bound.
Values may be sent and summed in bfloat16 or wider, within the bound.
No kernel may reach another device: no remote copies, remote signals or barrier semaphores. Data moves between devices by JAX's collectives and lax.ppermute only.
A program may use at most 64 MiB of HBM per device.

v0:
```python
import math
import jax
import jax.numpy as jnp
from jax import lax
from jax.sharding import PartitionSpec as P

M = 576
N = 6144
ITERS = 2
coef_a = 3.4445
coef_b = -4.775
coef_c = 2.0315
decay = 0.95
eps = 1e-07


def per_device(grad, momentum, owner):
    new_momentum = decay * momentum + grad.astype(jnp.float32)
    direction = grad.astype(jnp.float32) + decay * new_momentum
    total = lax.psum(jnp.sum(direction * direction), "tensor")
    rows_here = (direction[0] / (jnp.sqrt(total) + eps)).astype(jnp.bfloat16)
    columns = lax.all_to_all(rows_here, "tensor", split_axis=1, concat_axis=0, tiled=True)
    for step in range(ITERS):
        gram = lax.psum(
            jnp.dot(columns, columns.T, preferred_element_type=jnp.float32), "tensor"
        ).astype(jnp.bfloat16)
        square = jnp.dot(gram, gram, preferred_element_type=jnp.float32)
        poly = (coef_b * gram.astype(jnp.float32) + coef_c * square).astype(jnp.bfloat16)
        applied = jnp.dot(poly, columns, preferred_element_type=jnp.float32)
        columns = (coef_a * columns.astype(jnp.float32) + applied).astype(jnp.bfloat16)
    factor = 0.2 * math.sqrt(max(M, N))
    back_rows = lax.all_to_all(columns, "tensor", split_axis=0, concat_axis=1, tiled=True)
    scaled = (factor * back_rows.astype(jnp.float32)).astype(jnp.bfloat16)
    every_slot = lax.all_gather(scaled[None], "dp", axis=0, tiled=True)
    matrix_ids = jnp.arange(every_slot.shape[0], dtype=jnp.int32)
    selector = (owner[None, :] == matrix_ids[:, None]).astype(jnp.bfloat16)
    update = jnp.einsum(
        "mg,grn->mrn", selector, every_slot, preferred_element_type=jnp.float32
    ).astype(jnp.bfloat16)
    return (update, new_momentum)


def solution(mesh):
    in_specs = (P("dp", "tensor", None), P("dp", "tensor", None), P())
    out_specs = (P(None, "tensor", None), P("dp", "tensor", None))
    return jax.shard_map(
        per_device, mesh=mesh, in_specs=in_specs, out_specs=out_specs, check_vma=False
    )
```

profile of v0, /device:TPU:0, one launch (start us, length us, event | category | flops | bytes accessed | tf_op | source)
XLA Modules:
  0.0 286.8 jit_solution(11792428714496908145)
XLA Ops:
  7.2 0.0 copy-start.1
  7.2 0.0 all-gather.2.cloned.1.call-start
  7.2 2.9 %multiply_reduce_fusion = (f32[]{:T(128)}, f32[1,72,6144]{2,1,0:T(8,128)S(1)}) fusion(bf16[1,72,6144]{2,1,0:T(8,128)(2,1)} %param.3, f32[1,72,6144]{2,1,0:T(8,128)} %param.4), kind=kLoop, calls=%fused_computation.8 | loop fusion | flops 3096575 | bytes 4423684 | tf_op jit(solution)/shard_map/reduce_sum | solution.py:20
  10.1 0.0 copy-start
  10.1 23.8 %psum.21 = f32[]{:T(128)} all-reduce(f32[]{:T(128)} %get-tuple-element.8), channel_id=1, replica_groups=mesh['dp'=4,'tensor'=8] {'tensor'}, use_global_device_ids=true, to_apply=%region_1.0 | all-reduce | flops 1 | bytes 8 | tf_op jit(solution)/shard_map/psum | solution.py:20
  34.6 0.0 copy-done.1
  34.6 0.3 divide_convert_fusion
  34.8 0.0 copy-done
  34.9 0.2 copy.16
  35.0 0.2 copy.12
  35.2 21.7 %all_to_all.29 = bf16[72,8,768]{2,0,1:T(8,128)(2,1)S(1)} all-to-all(bf16[72,8,768]{2,0,1:T(8,128)(2,1)S(1)} %copy.12), channel_id=1, replica_groups=mesh['dp'=4,'tensor'=8] {'tensor'}, dimensions={1} | all-to-all | bytes 1769472 | tf_op jit(solution)/shard_map/all_to_all | solution.py:22
  56.9 0.9 fusion.17
  57.7 79.9 %all-reduce.2 = bf16[576,576]{1,0:T(8,128)(2,1)S(1)} all-reduce(f32[576,576]{1,0:T(8,128)S(1)} %fusion.17), channel_id=1, replica_groups=mesh['dp'=4,'tensor'=8] {'tensor'}, use_global_device_ids=true, to_apply=%region_2.0 | all-reduce | flops 331776 | bytes 1990656 | tf_op jit(solution)/shard_map/psum | solution.py:24
  137.6 1.6 add_convert_fusion.1
  139.3 0.0 copy-start.3
  139.3 0.9 copy-done.3
  140.2 0.9 fusion.18
  141.1 0.0 copy-start.4
  141.1 78.1 %all-reduce.3 = bf16[576,576]{1,0:T(8,128)(2,1)S(1)} all-reduce(f32[576,576]{1,0:T(8,128)S(1)} %fusion.18), channel_id=1, replica_groups=mesh['dp'=4,'tensor'=8] {'tensor'}, use_global_device_ids=true, to_apply=%region_3.0 | all-reduce | flops 331776 | bytes 1990656 | tf_op jit(solution)/shard_map/psum | solution.py:24
  219.2 0.0 copy-done.4
  219.2 1.6 add_convert_fusion
  220.8 18.7 %all_to_all.30 = bf16[8,72,768]{2,1,0:T(8,128)(2,1)S(1)} all-to-all(bf16[8,72,768]{2,1,0:T(8,128)(2,1)S(1)} %bitcast.26), channel_id=1, replica_groups=mesh['dp'=4,'tensor'=8] {'tensor'}, dimensions={0} | all-to-all | bytes 1769472 | tf_op jit(solution)/shard_map/all_to_all | solution.py:32
  239.6 0.2 fusion.1
  239.7 0.2 copy.13
  239.9 0.0 copy-start.2
  239.9 1.3 convert_element_type.89
  241.2 0.0 all-gather.2.cloned.1.call-update
  241.2 28.5 %all-gather.2.cloned.1.call-done = bf16[4,72,6144]{2,1,0:T(8,128)(2,1)} async-done(((bf16[1,72,6144]{2,1,0:T(8,128)(2,1)}), bf16[4,72,6144]{2,1,0:T(8,128)(2,1)}) %all-gather.2.cloned.1.call-update) | async-done | bytes 3538960 | tf_op jit(solution)/shard_map/all_gather | solution.py:34
  269.7 0.0 copy-done.2
  269.7 6.5 %convolution_convert_fusion = bf16[4,72,6144]{2,0,1:T(4,128)(2,1)S(1)} fusion(bf16[4,72,6144]{2,1,0:T(8,128)(2,1)} %all-gather.2.cloned.1.call-done, s32[4]{0:T(128)S(1)} %copy-done.2), kind=kOutput, calls=%fused_computation | convolution fusion | flops 15925264 | bytes 7077904 | tf_op jit(solution)/shard_map/mg,grn->mrn/dot_general | solution.py:37
  276.2 3.7 %copy.15 = bf16[4,72,6144]{2,1,0:T(8,128)(2,1)} copy(bf16[4,72,6144]{2,0,1:T(4,128)(2,1)S(1)} %convolution_convert_fusion) | data formatting | bytes 7077888
Async XLA Ops:
  7.2 27.4 %copy-start.1 = (bf16[1,72,6144]{2,1,0:T(8,128)(2,1)S(1)}, bf16[1,72,6144]{2,1,0:T(8,128)(2,1)}, u32[]{:S(2)}) copy-start(bf16[1,72,6144]{2,1,0:T(8,128)(2,1)} %param.3) | copy-start | bytes 2654212
  7.2 262.5 %all-gather.2.cloned.1.call-start = ((), (), s32[]{:S(2)}) async-start(), calls=%async_computation.2 | async-start | bytes 4423680 | tf_op jit(solution)/shard_map/all_gather | solution.py:34
  10.1 24.7 %copy-start = (f32[1,72,6144]{2,1,0:T(8,128)}, f32[1,72,6144]{2,1,0:T(8,128)S(1)}, u32[]{:S(2)}) copy-start(f32[1,72,6144]{2,1,0:T(8,128)S(1)} %get-tuple-element.9) | copy-start | bytes 5308420
  139.3 0.9 copy-start.3
  141.1 78.1 %copy-start.4 = (bf16[576,768]{1,0:T(8,128)(2,1)S(1)}, bf16[576,768]{1,0:T(8,128)(2,1)}, u32[]{:S(2)}) copy-start(bf16[576,768]{1,0:T(8,128)(2,1)} %copy-done.3) | copy-start | bytes 2654212
  239.9 29.8 %copy-start.2 = (s32[4]{0:T(128)S(1)}, s32[4]{0:T(128)}, u32[]{:S(2)}) copy-start(s32[4]{0:T(128)} %param.5) | copy-start | bytes 52
Sparse Core Ops, SparseCore 0:
  241.3 28.2 all-gather.1
where the time goes:
time: 287 us
  blocking collectives  222 us (77%)
  waiting for transfers between devices  28.5 us (10%)
  between operations  14.8 us (5%)
  matrix products  11.6 us (4%)
  local copies, waits for them, and re-layouts  6.44 us (2%)
  other arithmetic  3.29 us (1%)
    psum x2, blocking collectives, per_device(): lax.psum(jnp.dot(columns, columns.T, preferred_element_type=jnp.float32),...  158 us
    all_gather x1, waiting for transfers between devices, per_device(): every_slot = lax.all_gather(scaled[None], 'dp', axis=0, tiled=True)  28.5 us
    psum x1, blocking collectives, per_device(): total = lax.psum(jnp.sum(direction * direction), 'tensor')  23.8 us
    all_to_all x1, blocking collectives, per_device(): lax.all_to_all(rows_here, 'tensor', split_axis=1, concat_axis=0, tiled=True)  21.7 us
    all_to_all x1, blocking collectives, per_device(): lax.all_to_all(columns, 'tensor', split_axis=0, concat_axis=1, tiled=True)  18.7 us
    dot_general x1, matrix products, per_device(): jnp.einsum('mg,grn->mrn', selector, every_slot, preferred_element_type=jn...  6.52 us
  transfers between devices with their start and end apart: 1, of which 1 were waited for; matrix products, arithmetic and copies ran while one was open for 0% of the time, Pallas kernels for 0%

commit v1 on v0

--- a/solution.py
+++ b/solution.py
@@ -29,7 +29,19 @@
         applied = jnp.dot(poly, columns, preferred_element_type=jnp.float32)
         columns = (coef_a * columns.astype(jnp.float32) + applied).astype(jnp.bfloat16)
     factor = 0.2 * math.sqrt(max(M, N))
-    back_rows = lax.all_to_all(columns, "tensor", split_axis=0, concat_axis=1, tiled=True)
+    ways, here = (lax.axis_size("tensor"), lax.axis_index("tensor"))
+    width = columns.shape[0] // ways
+    shape = list(columns.shape)
+    shape[0] = width
+    height = shape[1]
+    shape[1] = height * ways
+    full = jnp.zeros(shape, columns.dtype)
+    for mask in range(ways):
+        part = lax.dynamic_slice_in_dim(columns, (here ^ mask) * width, width, axis=0)
+        if mask:
+            part = lax.ppermute(part, "tensor", [(d, d ^ mask) for d in range(ways)])
+        full = lax.dynamic_update_slice_in_dim(full, part, (here ^ mask) * height, axis=1)
+    back_rows = full
     scaled = (factor * back_rows.astype(jnp.float32)).astype(jnp.bfloat16)
     every_slot = lax.all_gather(scaled[None], "dp", axis=0, tiled=True)
     matrix_ids = jnp.arange(every_slot.shape[0], dtype=jnp.int32)

time: 287 us -> 293 us (1.021)
  blocking collectives: 222 us -> 180 us
  waiting for transfers between devices: 28.5 us -> 60.4 us
  starting transfers between devices: 0.04 us -> 14.1 us
    all_to_all x2 -> x0, blocking collectives: 40.4 us -> none  [the longest x1 21.7 us: per_device(): lax.all_to_all(rows_here, 'tensor', split_axis=1, concat_axis=0, tiled=True)]
    all_to_all x0 -> x1, waiting for transfers between devices: none -> 18.8 us  [per_device(): lax.all_to_all(rows_here, 'tensor', split_axis=1, concat_axis=0, tiled=True)]
    ppermute x0 -> x7, waiting for transfers between devices: none -> 10.6 us  [per_device(): part = lax.ppermute(part, 'tensor', [(d, d ^ mask) for d in range(ways)])]
    ppermute x0 -> x7, starting transfers between devices: none -> 10.5 us  [per_device(): part = lax.ppermute(part, 'tensor', [(d, d ^ mask) for d in range(ways)])]
    all_to_all x0 -> x1, starting transfers between devices: none -> 3.55 us  [per_device(): lax.all_to_all(rows_here, 'tensor', split_axis=1, concat_axis=0, tiled=True)]
  transfers between devices with their start and end apart: 1 -> 9, of which waited for: 1 -> 4; matrix products, arithmetic and copies ran while one was open for 0% -> 0% of each run, Pallas kernels for 0% -> 0%
where the time goes in v1:
time: 293 us; the launch traced here: 292 us
  blocking collectives  180 us (61%)
  waiting for transfers between devices  60.4 us (21%)
  between operations  15 us (5%)
  starting transfers between devices  14.1 us (5%)
  matrix products  13.1 us (4%)
  local copies, waits for them, and re-layouts  5.24 us (2%)
  other arithmetic  4.21 us (1%)
    psum x2, blocking collectives, per_device(): lax.psum(jnp.dot(columns, columns.T, preferred_element_type=jnp.float32),...  157 us
    all_gather x1, waiting for transfers between devices, per_device(): every_slot = lax.all_gather(scaled[None], 'dp', axis=0, tiled=True)  31 us
    psum x1, blocking collectives, per_device(): total = lax.psum(jnp.sum(direction * direction), 'tensor')  23.8 us
    all_to_all x1, waiting for transfers between devices, per_device(): lax.all_to_all(rows_here, 'tensor', split_axis=1, concat_axis=0, tiled=True)  18.8 us
    ppermute x7, waiting for transfers between devices, per_device(): part = lax.ppermute(part, 'tensor', [(d, d ^ mask) for d in range(ways)])  10.6 us
    ppermute x7, starting transfers between devices, per_device(): part = lax.ppermute(part, 'tensor', [(d, d ^ mask) for d in range(ways)])  10.5 us
    dot_general x1, matrix products, per_device(): jnp.einsum('mg,grn->mrn', selector, every_slot, preferred_element_type=jn...  6.52 us
  transfers between devices with their start and end apart: 9, of which 4 were waited for; matrix products, arithmetic and copies ran while one was open for 0% of the time, Pallas kernels for 0%

profile of v1, /device:TPU:0, one launch (start us, length us, event | category | flops | bytes accessed | tf_op | source)
XLA Modules:
  0.0 292.4 jit_solution(3061818345895533840)
XLA Ops:
  7.2 0.0 copy-start.1
  7.2 2.9 multiply_reduce_fusion
  10.1 0.0 copy-start
  10.1 23.8 %psum.21 = f32[]{:T(128)} all-reduce(f32[]{:T(128)} %get-tuple-element.6), channel_id=1, replica_groups=mesh['dp'=4,'tensor'=8] {'tensor'}, use_global_device_ids=true, to_apply=%region_1.0 | all-reduce | flops 1 | bytes 8 | tf_op jit(solution)/shard_map/psum | solution.py:20
  34.5 0.0 copy-done.1
  34.5 0.3 divide_convert_fusion
  34.8 0.0 copy-done
  34.8 0.2 copy.10
  35.0 1.1 copy.7
  36.0 3.6 %all-to-all-start = ((bf16[72,8,768]{2,0,1:T(8,128)(2,1)}), bf16[72,8,768]{2,0,1:T(8,128)(2,1)S(1)}, u32[]{:S(2)}, u32[]{:S(2)}) async-start(bf16[72,8,768]{2,0,1:T(8,128)(2,1)} %copy.7), calls=%async_computation | async-start | bytes 1769472 | tf_op jit(solution)/shard_map/all_to_all | solution.py:22
  39.6 0.0 all-gather.3.cloned.1.call-start
  39.7 18.8 %all-to-all-done = bf16[72,8,768]{2,0,1:T(8,128)(2,1)S(1)} async-done(((bf16[72,8,768]{2,0,1:T(8,128)(2,1)}), bf16[72,8,768]{2,0,1:T(8,128)(2,1)S(1)}, u32[]{:S(2)}, u32[]{:S(2)}) %all-to-all-start) | async-done | bytes 884768 | tf_op jit(solution)/shard_map/all_to_all | solution.py:22
  58.5 0.9 fusion.16
  59.4 78.3 %all-reduce.2 = bf16[576,576]{1,0:T(8,128)(2,1)S(1)} all-reduce(f32[576,576]{1,0:T(8,128)S(1)} %fusion.16), channel_id=1, replica_groups=mesh['dp'=4,'tensor'=8] {'tensor'}, use_global_device_ids=true, to_apply=%region_2.0 | all-reduce | flops 331776 | bytes 1990656 | tf_op jit(solution)/shard_map/psum | solution.py:24
  137.7 1.6 add_convert_fusion.1
  139.3 0.0 copy-start.3
  139.4 0.9 fusion.17
  140.2 0.0 copy-done.3
  140.3 78.4 %all-reduce.3 = bf16[576,576]{1,0:T(8,128)(2,1)S(1)} all-reduce(f32[576,576]{1,0:T(8,128)S(1)} %fusion.17), channel_id=1, replica_groups=mesh['dp'=4,'tensor'=8] {'tensor'}, use_global_device_ids=true, to_apply=%region_3.0 | all-reduce | flops 331776 | bytes 1990656 | tf_op jit(solution)/shard_map/psum | solution.py:24
  218.7 3.1 %add_convert_fusion = bf16[576,768]{1,0:T(8,128)(2,1)S(1)} fusion(bf16[576,768]{1,0:T(8,128)(2,1)} %copy-done.3, bf16[576,576]{1,0:T(8,128)(2,1)S(1)} %all-reduce.3), kind=kOutput, calls=%fused_computation.5 | convolution fusion | flops 895242240 | bytes 2433024 | tf_op jit(solution)/shard_map/dot_general | solution.py:29
  221.8 0.1 broadcast_in_dim.8
  221.9 0.1 constant_dynamic-slice_fusion
  222.0 2.2 collective-permute-start
  224.2 2.4 collective-permute-start.6
  226.6 1.0 collective-permute-start.5
  227.6 3.0 %collective-permute-start.4 = (bf16[72,768]{1,0:T(8,128)(2,1)S(1)}, bf16[72,768]{1,0:T(8,128)(2,1)S(1)}, u32[]{:S(2)}, u32[]{:S(2)}) collective-permute-start(bf16[72,768]{1,0:T(8,128)(2,1)S(1)} %get-tuple-element.10), channel_id=1, source_target_pairs={{0,5},{1,4},{2,7},{3,6},{4,1},{5,0},{6,3},{7,2},{8,13},{9,12},{10,... | collective-permute-start | bytes 331784 | tf_op jit(solution)/shard_map/ppermute | solution.py:42
  230.6 1.2 collective-permute-start.3
  231.8 0.0 collective-permute-done
  231.8 0.7 collective-permute-start.1
  232.5 5.0 %collective-permute-done.1 = bf16[72,768]{1,0:T(8,128)(2,1)S(1)} collective-permute-done((bf16[72,768]{1,0:T(8,128)(2,1)S(1)}, bf16[72,768]{1,0:T(8,128)(2,1)S(1)}, u32[]{:S(2)}, u32[]{:S(2)}) %collective-permute-start.1) | collective-permute-done | bytes 110624 | tf_op jit(solution)/shard_map/ppermute | solution.py:42
  237.5 0.0 collective-permute-start.2
  237.5 5.6 %collective-permute-done.2 = bf16[72,768]{1,0:T(8,128)(2,1)S(1)} collective-permute-done((bf16[72,768]{1,0:T(8,128)(2,1)S(1)}, bf16[72,768]{1,0:T(8,128)(2,1)S(1)}, u32[]{:S(2)}, u32[]{:S(2)}) %collective-permute-start.2) | collective-permute-done | bytes 110624 | tf_op jit(solution)/shard_map/ppermute | solution.py:42
  243.1 0.0 copy-start.2
  243.2 0.0 collective-permute-done.3
  243.2 0.0 collective-permute-done.4
  243.2 0.0 collective-permute-done.5
  243.3 0.0 collective-permute-done.6
  243.3 1.1 multiply_convert_fusion
  244.4 0.0 all-gather.3.cloned.1.call-update
  244.4 31.0 %all-gather.3.cloned.1.call-done = bf16[288,6144]{1,0:T(8,128)(2,1)} async-done(((bf16[72,6144]{1,0:T(8,128)(2,1)}), bf16[288,6144]{1,0:T(8,128)(2,1)}) %all-gather.3.cloned.1.call-update) | async-done | bytes 3538960 | tf_op jit(solution)/shard_map/all_gather | solution.py:46
  275.3 0.0 copy-done.2
  275.3 6.5 %convolution_convert_fusion = bf16[4,72,6144]{2,0,1:T(4,128)(2,1)S(1)} fusion(bf16[4,72,6144]{2,1,0:T(8,128)(2,1)} %bitcast.24, s32[4]{0:T(128)S(1)} %copy-done.2), kind=kOutput, calls=%fused_computation | convolution fusion | flops 15925264 | bytes 7077904 | tf_op jit(solution)/shard_map/mg,grn->mrn/dot_general | solution.py:49
  281.9 3.7 %copy.9 = bf16[4,72,6144]{2,1,0:T(8,128)(2,1)} copy(bf16[4,72,6144]{2,0,1:T(4,128)(2,1)S(1)} %convolution_convert_fusion) | data formatting | bytes 7077888
  (7 shorter events, 0.1 us)
Async XLA Ops:
  7.2 27.4 %copy-start.1 = (bf16[1,72,6144]{2,1,0:T(8,128)(2,1)S(1)}, bf16[1,72,6144]{2,1,0:T(8,128)(2,1)}, u32[]{:S(2)}) copy-start(bf16[1,72,6144]{2,1,0:T(8,128)(2,1)} %param.3) | copy-start | bytes 2654212
  10.1 24.7 %copy-start = (f32[1,72,6144]{2,1,0:T(8,128)}, f32[1,72,6144]{2,1,0:T(8,128)S(1)}, u32[]{:S(2)}) copy-start(f32[1,72,6144]{2,1,0:T(8,128)S(1)} %get-tuple-element.7) | copy-start | bytes 5308420
  36.0 22.5 %all-to-all-start = ((bf16[72,8,768]{2,0,1:T(8,128)(2,1)}), bf16[72,8,768]{2,0,1:T(8,128)(2,1)S(1)}, u32[]{:S(2)}, u32[]{:S(2)}) async-start(bf16[72,8,768]{2,0,1:T(8,128)(2,1)} %copy.7), calls=%async_computation | async-start | bytes 1769472 | tf_op jit(solution)/shard_map/all_to_all | solution.py:22
  39.6 235.7 %all-gather.3.cloned.1.call-start = ((), (), s32[]{:S(2)}) async-start(), calls=%async_computation.1 | async-start | bytes 4423680 | tf_op jit(solution)/shard_map/all_gather | solution.py:46
  139.3 0.9 copy-start.3
  222.0 9.8 %collective-permute-start = (bf16[72,768]{1,0:T(8,128)(2,1)S(1)}, bf16[72,768]{1,0:T(8,128)(2,1)S(1)}, u32[]{:S(2)}, u32[]{:S(2)}) collective-permute-start(bf16[72,768]{1,0:T(8,128)(2,1)S(1)} %get-tuple-element.14), channel_id=1, source_target_pairs={{0,1},{1,0},{2,3},{3,2},{4,5},{5,4},{6,7},{7,6},{8,9},{9,8},{10,11... | collective-permute-start | bytes 331784 | tf_op jit(solution)/shard_map/ppermute | solution.py:42
  224.2 19.1 %collective-permute-start.6 = (bf16[72,768]{1,0:T(8,128)(2,1)S(1)}, bf16[72,768]{1,0:T(8,128)(2,1)S(1)}, u32[]{:S(2)}, u32[]{:S(2)}) collective-permute-start(bf16[72,768]{1,0:T(8,128)(2,1)S(1)} %get-tuple-element.8), channel_id=1, source_target_pairs={{0,7},{1,6},{2,5},{3,4},{4,3},{5,2},{6,1},{7,0},{8,15},{9,14},{10,... | collective-permute-start | bytes 331784 | tf_op jit(solution)/shard_map/ppermute | solution.py:42
  226.6 16.7 %collective-permute-start.5 = (bf16[72,768]{1,0:T(8,128)(2,1)S(1)}, bf16[72,768]{1,0:T(8,128)(2,1)S(1)}, u32[]{:S(2)}, u32[]{:S(2)}) collective-permute-start(bf16[72,768]{1,0:T(8,128)(2,1)S(1)} %get-tuple-element.9), channel_id=1, source_target_pairs={{0,6},{1,7},{2,4},{3,5},{4,2},{5,3},{6,0},{7,1},{8,14},{9,15},{10,... | collective-permute-start | bytes 331784 | tf_op jit(solution)/shard_map/ppermute | solution.py:42
  227.6 15.6 %collective-permute-start.4 = (bf16[72,768]{1,0:T(8,128)(2,1)S(1)}, bf16[72,768]{1,0:T(8,128)(2,1)S(1)}, u32[]{:S(2)}, u32[]{:S(2)}) collective-permute-start(bf16[72,768]{1,0:T(8,128)(2,1)S(1)} %get-tuple-element.10), channel_id=1, source_target_pairs={{0,5},{1,4},{2,7},{3,6},{4,1},{5,0},{6,3},{7,2},{8,13},{9,12},{10,... | collective-permute-start | bytes 331784 | tf_op jit(solution)/shard_map/ppermute | solution.py:42
  230.6 12.6 %collective-permute-start.3 = (bf16[72,768]{1,0:T(8,128)(2,1)S(1)}, bf16[72,768]{1,0:T(8,128)(2,1)S(1)}, u32[]{:S(2)}, u32[]{:S(2)}) collective-permute-start(bf16[72,768]{1,0:T(8,128)(2,1)S(1)} %get-tuple-element.11), channel_id=1, source_target_pairs={{0,4},{1,5},{2,6},{3,7},{4,0},{5,1},{6,2},{7,3},{8,12},{9,13},{10,... | collective-permute-start | bytes 331784 | tf_op jit(solution)/shard_map/ppermute | solution.py:42
  231.8 5.7 %collective-permute-start.1 = (bf16[72,768]{1,0:T(8,128)(2,1)S(1)}, bf16[72,768]{1,0:T(8,128)(2,1)S(1)}, u32[]{:S(2)}, u32[]{:S(2)}) collective-permute-start(bf16[72,768]{1,0:T(8,128)(2,1)S(1)} %get-tuple-element.13), channel_id=1, source_target_pairs={{0,2},{1,3},{2,0},{3,1},{4,6},{5,7},{6,4},{7,5},{8,10},{9,11},{10,... | collective-permute-start | bytes 331784 | tf_op jit(solution)/shard_map/ppermute | solution.py:42
  237.5 5.6 %collective-permute-start.2 = (bf16[72,768]{1,0:T(8,128)(2,1)S(1)}, bf16[72,768]{1,0:T(8,128)(2,1)S(1)}, u32[]{:S(2)}, u32[]{:S(2)}) collective-permute-start(bf16[72,768]{1,0:T(8,128)(2,1)S(1)} %get-tuple-element.12), channel_id=1, source_target_pairs={{0,3},{1,2},{2,1},{3,0},{4,7},{5,6},{6,5},{7,4},{8,11},{9,10},{10,... | collective-permute-start | bytes 331784 | tf_op jit(solution)/shard_map/ppermute | solution.py:42
  243.1 32.2 %copy-start.2 = (s32[4]{0:T(128)S(1)}, s32[4]{0:T(128)}, u32[]{:S(2)}) copy-start(s32[4]{0:T(128)} %param.5) | copy-start | bytes 52
Sparse Core Ops, SparseCore 0:
  244.5 30.7 all-gather.2
